TPU v7x, 32 devices: a whole 2x2x4 slice. The times are simulated.
32 devices in a mesh: groups: 2 (over y), ctx: 4 (over x, core), head: 4 (over z).
Axes of the slice: x: 2, y: 2, z: 4, core: 2. Of those that a mesh axis runs over, the one named last changes fastest.
Arguments:
- span_query: bfloat16 [4, 128, 64, 128], P('groups', 'ctx', 'head'), parts along dimension 0, may hold values from -5 to 5
- span_key: bfloat16 [4, 128, 8, 128], P('groups', 'ctx', 'head'), parts along dimension 0, may hold values from -15 to 15
- span_value: bfloat16 [4, 128, 8, 128], P('groups', 'ctx', 'head'), parts along dimension 0, may hold values from -6 to 6
- prefix_key: bfloat16 [64, 128, 8, 128], P(('groups', 'ctx'), None, 'head'), parts along dimension 0, may hold values from -15 to 15
- prefix_value: bfloat16 [64, 128, 8, 128], P(('groups', 'ctx'), None, 'head'), parts along dimension 0, may hold values from -6 to 6
- page_table: int32 [4, 16], P('groups', 'ctx'), parts along dimension 0, may hold values from 0 to 7, as said below
- decode_query: bfloat16 [8, 32, 64, 128], P('groups', 'ctx', 'head'), parts along dimension 0, may hold values from -5 to 5
- decode_key: bfloat16 [8, 32, 8, 128], P('groups', 'ctx', 'head'), parts along dimension 0, may hold values from -15 to 15
- decode_value: bfloat16 [8, 32, 8, 128], P('groups', 'ctx', 'head'), parts along dimension 0, may hold values from -6 to 6
- sample_prompt: int32 [64], P('groups'), parts along dimension 0, may hold values from 0 to 1, as said below
- out_weight: bfloat16 [8192, 8192], P('head', 'ctx'), may hold values from -0.25 to 0.25
Outputs:
- span_out: bfloat16 [4, 128, 8192], P('groups', None, 'ctx'), parts along dimension 0
- decode_out: bfloat16 [8, 32, 8192], P('groups', None, 'ctx'), parts along dimension 0
There are 2 independent parts, one for each index of `groups`. A program takes and returns all parts, laid end to end along the dimension named above; an argument that names none is the same for every part. Nothing has to cross between parts.
Inputs may be any that keep to these rules, and one draw needn't show every extreme that they name: `page_table`: within each block of 4 columns (one index of ctx) the entries of both prompts together are a permutation of 0 to 7. `sample_prompt`: every prompt has exactly 16 samples.
All inputs are finite; a program needn't handle non-finite values.
Results may differ from a plain program's by a relative error of at most 0.0075.
Values may be sent and summed in bfloat16 or wider, within the bound.
No kernel may reach another device: no remote copies, remote signals or barrier semaphores. Data moves between devices by JAX's collectives and lax.ppermute only.
A program may use at most 64 MiB of HBM per device.

v0:
```python
import math
import jax
import jax.numpy as jnp
from jax import lax
from jax.sharding import PartitionSpec as P

negative_floor = -1e30


def absorb(softmax_state, queries, key_rows, value_rows, allowed):
    running_max, running_sum, weighted = softmax_state
    scores = jnp.einsum("brd,bnd->brn", queries, key_rows, preferred_element_type=jnp.float32) * (
        1.0 / math.sqrt(queries.shape[-1])
    )
    if allowed is not None:
        scores = jnp.where(allowed, scores, negative_floor)
    new_max = jnp.maximum(running_max, jnp.max(scores, axis=-1))
    factor = jnp.exp(running_max - new_max)
    weights = jnp.exp(scores - new_max[..., None])
    running_sum = running_sum * factor + jnp.sum(weights, axis=-1)
    weighted = weighted * factor[..., None] + jnp.einsum(
        "brn,bnd->brd", weights.astype(jnp.bfloat16), value_rows, preferred_element_type=jnp.float32
    )
    return (new_max, running_sum, weighted)


def sweep(softmax_state, queries, key_rows, value_rows, block_width):
    total_keys = key_rows.shape[1]
    block_width = math.gcd(total_keys, block_width)

    def one_block(state_in, block_start):
        key_block = lax.dynamic_slice_in_dim(key_rows, block_start, block_width, 1)
        value_block = lax.dynamic_slice_in_dim(value_rows, block_start, block_width, 1)
        return (absorb(state_in, queries, key_block, value_block, None), None)

    starts = jnp.arange(total_keys // block_width, dtype=jnp.int32) * block_width
    softmax_state, unused = lax.scan(one_block, softmax_state, starts)
    return softmax_state


def empty_state(head_batch, row_count, head_depth):
    return (
        jnp.full((head_batch, row_count), negative_floor, jnp.float32),
        jnp.zeros((head_batch, row_count), jnp.float32),
        jnp.zeros((head_batch, row_count, head_depth), jnp.float32),
    )


def own_steps(softmax_state, queries_five, own_key, own_value):
    running_max, running_sum, weighted = softmax_state
    key_rows = own_key.transpose(2, 1, 0, 3)
    value_rows = own_value.transpose(2, 1, 0, 3)
    scores = jnp.einsum(
        "ktsgd,ksud->ktsgu", queries_five, key_rows, preferred_element_type=jnp.float32
    ) * (1.0 / math.sqrt(queries_five.shape[-1]))
    step_total = queries_five.shape[1]
    step_ids = jnp.arange(step_total, dtype=jnp.int32)
    allowed = (step_ids[None, :] <= step_ids[:, None])[None, :, None, None, :]
    scores = jnp.where(allowed, scores, negative_floor)
    new_max = jnp.maximum(running_max, jnp.max(scores, axis=-1))
    factor = jnp.exp(running_max - new_max)
    weights = jnp.exp(scores - new_max[..., None])
    running_sum = running_sum * factor + jnp.sum(weights, axis=-1)
    weighted = weighted * factor[..., None] + jnp.einsum(
        "ktsgu,ksud->ktsgd",
        weights.astype(jnp.bfloat16),
        value_rows,
        preferred_element_type=jnp.float32,
    )
    return (weighted / running_sum[..., None]).astype(jnp.bfloat16)


def shards(
    span_query,
    span_key,
    span_value,
    prefix_key,
    prefix_value,
    page_table,
    decode_query,
    decode_key,
    decode_value,
    sample_prompt,
    out_weight,
):
    prompts, span_dev, heads_dev, head_depth = span_query.shape
    kv_heads = span_key.shape[2]
    group_size = heads_dev // kv_heads
    steps_count = decode_query.shape[0]
    samples_dev = decode_query.shape[1]
    head_batch = prompts * kv_heads
    ctx_index = lax.axis_index("ctx")
    slot_rows = page_table.reshape(-1)
    local_keys = (
        jnp.take(prefix_key, slot_rows, axis=0)
        .reshape(prompts, -1, kv_heads, head_depth)
        .transpose(0, 2, 1, 3)
    )
    local_values = (
        jnp.take(prefix_value, slot_rows, axis=0)
        .reshape(prompts, -1, kv_heads, head_depth)
        .transpose(0, 2, 1, 3)
    )
    span_rows = (
        span_query.reshape(prompts, span_dev, kv_heads, group_size, head_depth)
        .transpose(0, 2, 1, 3, 4)
        .reshape(head_batch, span_dev * group_size, head_depth)
    )
    span_keys_all, span_values_all = (
        lax.all_gather(span_key, "ctx", axis=1, tiled=True),
        lax.all_gather(span_value, "ctx", axis=1, tiled=True),
    )
    span_total = span_keys_all.shape[1]
    span_key_rows = span_keys_all.transpose(0, 2, 1, 3).reshape(head_batch, span_total, head_depth)
    span_value_rows = span_values_all.transpose(0, 2, 1, 3).reshape(
        head_batch, span_total, head_depth
    )
    query_pos = (
        ctx_index * span_dev + jnp.arange(span_dev * group_size, dtype=jnp.int32) // group_size
    )
    causal = (jnp.arange(span_total, dtype=jnp.int32)[None, :] <= query_pos[:, None])[None]
    decode_five = decode_query.reshape(
        steps_count, samples_dev, kv_heads, group_size, head_depth
    ).transpose(2, 0, 1, 3, 4)
    prefill_state = empty_state(head_batch, span_dev * group_size, head_depth)
    prompt_keys_all, prompt_values_all = (
        lax.all_gather(local_keys, "ctx", axis=2, tiled=True),
        lax.all_gather(local_values, "ctx", axis=2, tiled=True),
    )
    prefix_len = prompt_keys_all.shape[2]
    key_rows = prompt_keys_all.reshape(head_batch, prefix_len, head_depth)
    value_rows = prompt_values_all.reshape(head_batch, prefix_len, head_depth)
    prefill_state = sweep(prefill_state, span_rows, key_rows, value_rows, 2048)
    decode_flat = decode_five.reshape(kv_heads, -1, head_depth)
    decode_batch = jnp.broadcast_to(decode_flat[None], (prompts,) + decode_flat.shape).reshape(
        head_batch, -1, head_depth
    )
    decode_state = empty_state(head_batch, decode_flat.shape[1], head_depth)
    decode_state = sweep(decode_state, decode_batch, key_rows, value_rows, 2048)
    decode_state = sweep(decode_state, decode_batch, span_key_rows, span_value_rows, span_total)
    own_prompts = lax.dynamic_slice_in_dim(sample_prompt, ctx_index * samples_dev, samples_dev)
    chosen = (
        own_prompts[None, None, None, :, None]
        == jnp.arange(prompts, dtype=jnp.int32)[:, None, None, None, None]
    )

    def select_prompt(member):
        shaped = member.reshape(
            (prompts, kv_heads, steps_count, samples_dev, group_size) + member.shape[2:]
        )
        select_mask = chosen.reshape(chosen.shape + (1,) * (shaped.ndim - 5))
        return jnp.sum(jnp.where(select_mask, shaped, 0.0), axis=0)

    decode_state = tuple((select_prompt(member) for member in decode_state))
    prefill_state = absorb(prefill_state, span_rows, span_key_rows, span_value_rows, causal)
    span_mixed = (prefill_state[2] / prefill_state[1][..., None]).astype(jnp.bfloat16)
    span_attn = (
        span_mixed.reshape(prompts, kv_heads, span_dev, group_size, head_depth)
        .transpose(0, 2, 1, 3, 4)
        .reshape(prompts * span_dev, heads_dev * head_depth)
    )
    decode_mixed = own_steps(decode_state, decode_five, decode_key, decode_value)
    decode_attn = decode_mixed.transpose(1, 2, 0, 3, 4).reshape(
        steps_count * samples_dev, heads_dev * head_depth
    )
    rows_local = jnp.concatenate([span_attn, decode_attn], axis=0)
    projected = jnp.dot(
        lax.all_gather(rows_local, "ctx", axis=0, tiled=True),
        out_weight,
        preferred_element_type=jnp.float32,
    )
    share = lax.psum_scatter(projected, "head", scatter_dimension=0, tiled=True).astype(
        jnp.bfloat16
    )
    summed = lax.all_gather(share, "head", axis=0, tiled=True)
    rows_dev = rows_local.shape[0]
    blocks_by_ctx = summed.reshape(-1, rows_dev, summed.shape[-1])
    ctx_count = blocks_by_ctx.shape[0]
    span_out = (
        blocks_by_ctx[:, : prompts * span_dev]
        .reshape(ctx_count, prompts, span_dev, -1)
        .transpose(1, 0, 2, 3)
        .reshape(prompts, ctx_count * span_dev, -1)
    )
    decode_out = (
        blocks_by_ctx[:, prompts * span_dev :]
        .reshape(ctx_count, steps_count, samples_dev, -1)
        .transpose(1, 0, 2, 3)
        .reshape(steps_count, ctx_count * samples_dev, -1)
    )
    return (span_out, decode_out)


def solution(mesh):
    return jax.shard_map(
        shards,
        mesh=mesh,
        in_specs=(
            P("groups", "ctx", "head", None),
            P("groups", "ctx", "head", None),
            P("groups", "ctx", "head", None),
            P(("groups", "ctx"), None, "head", None),
            P(("groups", "ctx"), None, "head", None),
            P("groups", "ctx"),
            P("groups", "ctx", "head", None),
            P("groups", "ctx", "head", None),
            P("groups", "ctx", "head", None),
            P("groups"),
            P("head", "ctx"),
        ),
        out_specs=(P("groups", None, "ctx"), P("groups", None, "ctx")),
        check_vma=False,
    )
```

profile of v0, /device:TPU:0, one launch (start us, length us, event | category | flops | bytes accessed | tf_op | source)
XLA Modules:
  0.0 230.2 jit_solution(950019936043663763)
XLA Ops:
  7.2 0.0 copy-start
  7.2 0.0 copy-start.8
  7.2 0.0 all-gather.5.cloned.1.call-start
  7.3 0.8 reshape.229
  8.1 0.2 copy-done
  8.3 1.6 gather_fusion
  9.9 2.6 %gather_fusion.1 = bf16[8,128,2,128]{3,2,1,0:T(2,128)(2,1)S(1)} fusion(bf16[8,128,2,128]{3,2,1,0:T(2,128)(2,1)} %param.17, s32[1024]{0:T(1024)S(1)} %pad_clamp_fusion), kind=kCustom, calls=%fused_computation.1.clone | custom fusion | bytes 1048608 | tf_op jit(solution)/shard_map/jit(_take)/gather | solution.py:100
  12.6 1.0 broadcast_select_fusion.1
  13.6 0.9 copy.135
  14.4 0.0 all-gather.5.cloned.1.call-update
  14.5 0.0 all-gather.7.cloned.1.call-start
  14.5 0.9 copy.134
  15.4 0.0 all-gather.7.cloned.1.call-update
  15.4 0.0 all-gather.9.cloned.1.call-start
  15.5 6.7 %all_gather.20 = bf16[2,128,2,128]{3,2,1,0:T(2,128)(2,1)S(1)} all-gather(bf16[2,32,2,128]{3,2,1,0:T(2,128)(2,1)} %param.14), channel_id=1, replica_groups=mesh['groups'=2,'ctx'=4,'head'=4] {'ctx'}, dimensions={1}, use_global_device_ids=true | all-gather | bytes 163840 | tf_op jit(solution)/shard_map/all_gather | solution.py:110
  22.2 0.9 copy.89
  23.2 0.2 fusion.56
  23.4 6.2 %all_gather.21 = bf16[2,128,2,128]{3,2,1,0:T(2,128)(2,1)S(1)} all-gather(bf16[2,32,2,128]{3,2,1,0:T(2,128)(2,1)S(1)} %copy-done.9), channel_id=1, replica_groups=mesh['groups'=2,'ctx'=4,'head'=4] {'ctx'}, dimensions={1}, use_global_device_ids=true | all-gather | bytes 163840 | tf_op jit(solution)/shard_map/all_gather | solution.py:111
  29.8 0.7 reduce_max.56
  30.5 0.1 dynamic_slice.22
  30.6 0.5 iota_compare_fusion.2
  31.1 2.0 fusion.57
  33.0 0.2 fusion.58
  33.3 7.3 %all-gather.5.cloned.1.call-done = bf16[2,2,2048,128]{3,2,1,0:T(8,128)(2,1)} async-done(((bf16[2,2,512,128]{3,2,1,0:T(8,128)(2,1)}), bf16[2,2,2048,128]{3,2,1,0:T(8,128)(2,1)}) %all-gather.5.cloned.1.call-update) | async-done | bytes 2097168 | tf_op jit(solution)/shard_map/all_gather | solution.py:127
  40.6 2.9 %bitcast_reduce_fusion.1 = (f32[4,256]{1,0:T(4,128)S(1)}, f32[4,2048,256]{2,1,0:T(8,128)S(1)}) fusion(bf16[4,2048,128]{2,1,0:T(8,128)(2,1)} %bitcast.123, bf16[4,256,128]{2,1,0:T(8,128)(2,1)S(1)} %bitcast.131), kind=kOutput, calls=%fused_computation.6 | convolution fusion | flops 541064192 | bytes 10752000 | tf_op jit(solution)/shard_map/while/body/eval_jaxpr/brd,bnd->brn/dot_general | solution.py:12
  43.5 0.1 fusion.34
  43.6 3.4 %copy-done.1 = f32[4,2048,256]{2,1,0:T(8,128)} copy-done((f32[4,2048,256]{2,1,0:T(8,128)}, f32[4,2048,256]{2,1,0:T(8,128)S(1)}, u32[]{:S(2)}) %copy-start.1) | copy-done | bytes 8388632
  47.0 1.4 fusion.2
  48.4 0.6 multiply_add_fusion
  49.0 5.1 %bitcast_reduce_fusion = (f32[4,256]{1,0:T(4,128)}, f32[4,2048,256]{2,1,0:T(8,128)}) fusion(bf16[4,2048,128]{2,1,0:T(8,128)(2,1)S(1)} %bitcast.124, bf16[4,256,128]{2,1,0:T(8,128)(2,1)S(1)} %bitcast.129), kind=kOutput, calls=%fused_computation.3 | convolution fusion | flops 541064192 | bytes 10752000 | tf_op jit(solution)/shard_map/while/body/eval_jaxpr/brd,bnd->brn/dot_general | solution.py:12
  54.1 11.3 %all-gather.7.cloned.1.call-done = bf16[2,2,2048,128]{3,2,1,0:T(8,128)(2,1)} async-done(((bf16[2,2,512,128]{3,2,1,0:T(8,128)(2,1)}), bf16[2,2,2048,128]{3,2,1,0:T(8,128)(2,1)}) %all-gather.7.cloned.1.call-update) | async-done | bytes 2097168 | tf_op jit(solution)/shard_map/all_gather | solution.py:128
  65.4 5.2 %fusion.25 = f32[4,256,128]{2,1,0:T(8,128)S(1)} fusion(bf16[4,2048,128]{2,1,0:T(8,128)(2,1)} %bitcast.125, f32[4,2048,256]{2,1,0:T(8,128)} %copy-done.1, f32[4,256]{1,0:T(4,128)S(1)} %get-tuple-element.62, f32[4,256]{1,0:T(4,128)S(1)} %get-tuple-element.48, f32[4,256]{1,0:T(4,128)S(1)} %get-tuple-element.60), kind=kOutput, calls=%fused_computation.27 | convolution fusion | flops 543424512 | bytes 11022336 | tf_op jit(solution)/shard_map/while/body/eval_jaxpr/brn,bnd->brd/dot_general | solution.py:21
  70.6 0.3 fusion.28
  71.0 0.7 copy.136
  71.7 1.1 reshape.239
  72.8 1.3 fusion.54
  74.1 0.7 max.91
  74.8 4.8 %fusion.4 = f32[4,256]{1,0:T(4,128)S(1)} fusion(f32[4,2048,256]{2,1,0:T(8,128)} %get-tuple-element.84, f32[4,256]{1,0:T(4,128)S(1)} %get-tuple-element.71), kind=kLoop, calls=%fused_computation.10 | loop fusion | flops 6290432 | bytes 8396800 | tf_op jit(solution)/shard_map/while/body/eval_jaxpr/reduce_sum | solution.py:20
  79.5 0.7 reduce_sum.94
  80.3 0.1 fusion.36
  80.3 0.7 reduce_sum.96
  81.1 1.1 select_reduce_fusion.1
  82.1 0.8 copy_maximum_fusion
  82.9 1.0 fusion.43
  83.9 0.8 bitcast_add_fusion
  84.8 4.6 %fusion.22 = f32[4,256,128]{2,1,0:T(8,128)S(1)} fusion(bf16[4,2048,128]{2,1,0:T(8,128)(2,1)S(1)} %bitcast.126, f32[4,2048,256]{2,1,0:T(8,128)} %get-tuple-element.84, f32[4,256]{1,0:T(4,128)S(1)} %get-tuple-element.71, f32[4,256]{1,0:T(4,128)S(1)} %get-tuple-element.59, f32[4,256]{1,0:T(4,128)} %get-tuple-element.70), kind=kOutput, calls=%fused_computation.26 | convolution fusion | flops 543424512 | bytes 11022336 | tf_op jit(solution)/shard_map/while/body/eval_jaxpr/brn,bnd->brd/dot_general | solution.py:21
  89.3 0.3 convolution_add_fusion
  89.6 0.1 select_reduce_fusion
  89.8 0.3 fusion.31
  90.1 0.1 reshape.243
  90.2 0.8 pad_maximum_fusion
  91.0 0.0 all-gather.9.cloned.1.call-update
  91.0 0.3 reduce-scatter.2.cloned.1.call-start
  91.3 19.5 %all-gather.9.cloned.1.call-done = bf16[384,2048]{1,0:T(8,128)(2,1)} async-done(((bf16[96,2048]{1,0:T(8,128)(2,1)}), bf16[384,2048]{1,0:T(8,128)(2,1)}) %all-gather.9.cloned.1.call-update) | async-done | bytes 1572880 | tf_op jit(solution)/shard_map/all_gather | solution.py:168
  110.8 8.9 %fusion.59 = f32[384,2048]{1,0:T(8,128)} fusion(bf16[384,2048]{1,0:T(8,128)(2,1)} %all-gather.9.cloned.1.call-done, bf16[2048,2048]{1,0:T(8,128)(2,1)} %param.23), kind=kOutput, calls=%fused_computation.93 | convolution fusion | flops 3221225472 | bytes 13107200 | tf_op jit(solution)/shard_map/dot_general | solution.py:167
  119.7 0.0 reduce-scatter.2.cloned.1.call-update
  119.8 0.0 all-gather.11.cloned.1.call-start
  119.8 60.4 %reduce-scatter.2.cloned.1.call-done = f32[96,2048]{1,0:T(8,128)} async-done(((f32[384,2048]{1,0:T(8,128)}), f32[96,2048]{1,0:T(8,128)}) %reduce-scatter.2.cloned.1.call-update) | async-done | bytes 786448 | tf_op jit(solution)/shard_map/reduce_scatter | solution.py:172
  180.2 1.9 convert_element_type.35
  182.1 0.0 all-gather.11.cloned.1.call-update
  182.1 37.3 %all-gather.11.cloned.1.call-done = bf16[384,2048]{1,0:T(8,128)(2,1)} async-done(((bf16[96,2048]{1,0:T(8,128)(2,1)}), bf16[384,2048]{1,0:T(8,128)(2,1)}) %all-gather.11.cloned.1.call-update) | async-done | bytes 1572880 | tf_op jit(solution)/shard_map/all_gather | solution.py:175
  219.4 1.3 slice.12
  220.7 1.9 copy_bitcast_fusion
  222.6 1.0 copy.103
  (41 shorter events, 0.3 us)
Async XLA Ops:
  7.2 1.2 copy-start
  7.2 23.9 %copy-start.8 = (bf16[4,8,16,128]{3,2,1,0:T(8,128)(2,1)S(1)}, bf16[4,8,16,128]{3,2,1,0:T(8,128)(2,1)}, u32[]{:S(2)}) copy-start(bf16[4,8,16,128]{3,2,1,0:T(8,128)(2,1)} %param.19) | copy-start | bytes 393220
  7.2 16.2 %copy-start.9 = (bf16[2,32,2,128]{3,2,1,0:T(2,128)(2,1)S(1)}, bf16[2,32,2,128]{3,2,1,0:T(2,128)(2,1)}, u32[]{:S(2)}) copy-start(bf16[2,32,2,128]{3,2,1,0:T(2,128)(2,1)} %param.15) | copy-start | bytes 98308
  7.2 22.5 %copy-start.6 = (bf16[2,32,16,128]{3,2,1,0:T(8,128)(2,1)S(1)}, bf16[2,32,16,128]{3,2,1,0:T(8,128)(2,1)}, u32[]{:S(2)}) copy-start(bf16[2,32,16,128]{3,2,1,0:T(8,128)(2,1)} %param.13) | copy-start | bytes 786436
  7.2 23.3 %copy-start.14 = (s32[32]{0:T(128)S(1)}, s32[32]{0:T(128)}, u32[]{:S(2)}) copy-start(s32[32]{0:T(128)} %param.22) | copy-start | bytes 388
  7.2 23.9 %copy-start.12 = (bf16[4,8,2,128]{3,2,1,0:T(2,128)(2,1)S(1)}, bf16[4,8,2,128]{3,2,1,0:T(2,128)(2,1)}, u32[]{:S(2)}) copy-start(bf16[4,8,2,128]{3,2,1,0:T(2,128)(2,1)} %param.20) | copy-start | bytes 49156
  7.2 33.4 %all-gather.5.cloned.1.call-start = ((), (), s32[]{:S(2)}) async-start(), calls=%async_computation.1 | async-start | bytes 2621440 | tf_op jit(solution)/shard_map/all_gather | solution.py:127
  14.5 50.9 %all-gather.7.cloned.1.call-start = ((), (), s32[]{:S(2)}) async-start(), calls=%async_computation.2 | async-start | bytes 2621440 | tf_op jit(solution)/shard_map/all_gather | solution.py:128
  15.4 95.4 %all-gather.9.cloned.1.call-start = ((), (), s32[]{:S(2)}) async-start(), calls=%async_computation.3 | async-start | bytes 1966080 | tf_op jit(solution)/shard_map/all_gather | solution.py:168
  33.3 15.1 %copy-start.4 = (f32[4,256,128]{1,2,0:T(8,128)}, f32[4,256,128]{1,2,0:T(8,128)S(1)}, u32[]{:S(2)}) copy-start(f32[4,256,128]{1,2,0:T(8,128)S(1)} %get-tuple-element.90) | copy-start | bytes 1572868
  43.5 3.5 %copy-start.1 = (f32[4,2048,256]{2,1,0:T(8,128)}, f32[4,2048,256]{2,1,0:T(8,128)S(1)}, u32[]{:S(2)}) copy-start(f32[4,2048,256]{2,1,0:T(8,128)S(1)} %get-tuple-element.88) | copy-start | bytes 25165828
  43.5 5.5 %copy-start.2 = (bf16[2,2,2048,128]{3,2,1,0:T(8,128)(2,1)S(1)}, bf16[2,2,2048,128]{3,2,1,0:T(8,128)(2,1)}, u32[]{:S(2)}) copy-start(bf16[2,2,2048,128]{3,2,1,0:T(8,128)(2,1)} %all-gather.5.cloned.1.call-done) | copy-start | bytes 6291460
  54.1 16.6 %copy-start.10 = (f32[4,256]{1,0:T(4,128)S(1)}, f32[4,256]{1,0:T(4,128)}, u32[]{:S(2)}) copy-start(f32[4,256]{1,0:T(4,128)} %get-tuple-element.47) | copy-start | bytes 12292
  65.4 5.3 %copy-start.5 = (f32[4,256,128]{1,2,0:T(8,128)S(1)}, f32[4,256,128]{1,2,0:T(8,128)}, u32[]{:S(2)}) copy-start(f32[4,256,128]{1,2,0:T(8,128)} %copy-done.4) | copy-start | bytes 1572868
  70.6 14.2 %copy-start.3 = (bf16[2,2,2048,128]{3,2,1,0:T(8,128)(2,1)S(1)}, bf16[2,2,2048,128]{3,2,1,0:T(8,128)(2,1)}, u32[]{:S(2)}) copy-start(bf16[2,2,2048,128]{3,2,1,0:T(8,128)(2,1)} %all-gather.7.cloned.1.call-done) | copy-start | bytes 6291460
  81.1 8.6 %copy-start.11 = (pred[2,8]{1,0:T(4,128)(4,1)S(1)}, pred[2,8]{1,0:T(4,128)(4,1)}, u32[]{:S(2)}) copy-start(pred[2,8]{1,0:T(4,128)(4,1)} %iota_compare_fusion.2) | copy-start | bytes 52
  81.1 8.7 %copy-start.7 = (f32[2,4,8,8,4]{3,4,1,2,0:T(4,128)S(1)}, f32[2,4,8,8,4]{3,4,1,2,0:T(4,128)}, u32[]{:S(2)}) copy-start(f32[2,4,8,8,4]{3,4,1,2,0:T(4,128)} %get-tuple-element.86) | copy-start | bytes 24580
  81.1 8.7 %copy-start.13 = (bf16[4,8,2,128]{3,2,1,0:T(2,128)(2,1)S(1)}, bf16[4,8,2,128]{3,2,1,0:T(2,128)(2,1)}, u32[]{:S(2)}) copy-start(bf16[4,8,2,128]{3,2,1,0:T(2,128)(2,1)} %param.21) | copy-start | bytes 49156
  91.0 89.2 %reduce-scatter.2.cloned.1.call-start = ((), (), s32[]{:S(2)}) async-start(), calls=%async_computation.4 | async-start | bytes 3932160 | tf_op jit(solution)/shard_map/reduce_scatter | solution.py:172
  119.8 99.6 %all-gather.11.cloned.1.call-start = ((), (), s32[]{:S(2)}) async-start(), calls=%async_computation.5 | async-start | bytes 1966080 | tf_op jit(solution)/shard_map/all_gather | solution.py:175
Sparse Core Ops, SparseCore 0:
  14.6 25.9 all-gather.4
  42.7 22.5 all-gather.6
  91.1 19.6 all-gather.8
  119.9 60.2 reduce-scatter.1
  182.2 37.1 all-gather.10
where the time goes:
time: 231 us; the launch traced here: 230 us
  waiting for transfers between devices  136 us (59%)
  matrix products  30 us (13%)
  local copies, waits for them, and re-layouts  20.6 us (9%)
  other arithmetic  16.2 us (7%)
  between operations  14.1 us (6%)
  blocking collectives  12.9 us (6%)
    reduce_scatter x1, waiting for transfers between devices, shards(): lax.psum_scatter(projected, 'head', scatter_dimension=0, tiled=True)  60.4 us
    all_gather x1, waiting for transfers between devices, shards(): summed = lax.all_gather(share, 'head', axis=0, tiled=True)  37.3 us
    all_gather x1, waiting for transfers between devices, shards(): lax.all_gather(rows_local, 'ctx', axis=0, tiled=True)  19.5 us
    all_gather x1, waiting for transfers between devices, shards(): lax.all_gather(local_values, 'ctx', axis=2, tiled=True)  11.3 us
    dot_general x4, matrix products, absorb(): jnp.einsum('brn,bnd->brd', weights.astype(jnp.bfloat16), value_rows, pref...  10.4 us
    dot_general x1, matrix products, shards(): jnp.dot(lax.all_gather(rows_local, 'ctx', axis=0, tiled=True), out_weight...  8.94 us
    dot_general x4, matrix products, absorb(): jnp.einsum('brd,bnd->brn', queries, key_rows, preferred_element_type=jnp....  8.4 us
    all_gather x1, waiting for transfers between devices, shards(): lax.all_gather(local_keys, 'ctx', axis=2, tiled=True)  7.31 us
  transfers between devices with their start and end apart: 5, of which 5 were waited for; matrix products, arithmetic and copies ran while one was open for 7% of the time, Pallas kernels for 0%

commit v1 on v0

--- a/solution.py
+++ b/solution.py
@@ -5,6 +5,16 @@
 from jax.sharding import PartitionSpec as P
 
 negative_floor = -1e30
+
+
+def pass_along(x, mesh_axis, dim):
+    devices = lax.axis_size(mesh_axis)
+    block, blocks = (x, [x])
+    for _ in range(devices - 1):
+        block = lax.ppermute(block, mesh_axis, [(i, (i + 1) % devices) for i in range(devices)])
+        blocks.insert(0, block)
+    line = jnp.concatenate(blocks, axis=dim)
+    return jnp.roll(line, (lax.axis_index(mesh_axis) + 1) * x.shape[dim], axis=dim)
 
 
 def absorb(softmax_state, queries, key_rows, value_rows, allowed):
@@ -172,7 +182,7 @@
     share = lax.psum_scatter(projected, "head", scatter_dimension=0, tiled=True).astype(
         jnp.bfloat16
     )
-    summed = lax.all_gather(share, "head", axis=0, tiled=True)
+    summed = pass_along(share, "head", 0)
     rows_dev = rows_local.shape[0]
     blocks_by_ctx = summed.reshape(-1, rows_dev, summed.shape[-1])
     ctx_count = blocks_by_ctx.shape[0]

time: 231 us -> 224 us (0.970)
  local copies, waits for them, and re-layouts: 20.6 us -> 15.1 us
    all_gather x1 -> x0, waiting for transfers between devices: 37.3 us -> none  [shards(): summed = lax.all_gather(share, 'head', axis=0, tiled=True)]
    ppermute x0 -> x3, waiting for transfers between devices: none -> 33.7 us  [pass_along(): lax.ppermute(block, mesh_axis, [(i, (i + 1) % devices) for i in range(dev...]
    all_gather x1, waiting for transfers between devices: 11.3 us -> 14.2 us  [shards(): lax.all_gather(local_values, 'ctx', axis=2, tiled=True)]
  transfers between devices with their start and end apart: 5 -> 7, of which waited for: 5 -> 7; matrix products, arithmetic and copies ran while one was open for 7% -> 6% of each run, Pallas kernels for 0% -> 0%
where the time goes in v1:
time: 224 us; the launch traced here: 223 us
  waiting for transfers between devices  136 us (61%)
  matrix products  29.6 us (13%)
  local copies, waits for them, and re-layouts  15.1 us (7%)
  other arithmetic  14.5 us (6%)
  between operations  14.2 us (6%)
  blocking collectives  12.4 us (6%)
    reduce_scatter x1, waiting for transfers between devices, shards(): lax.psum_scatter(projected, 'head', scatter_dimension=0, tiled=True)  60.4 us
    ppermute x3, waiting for transfers between devices, pass_along(): lax.ppermute(block, mesh_axis, [(i, (i + 1) % devices) for i in range(dev...  33.7 us
    all_gather x1, waiting for transfers between devices, shards(): lax.all_gather(rows_local, 'ctx', axis=0, tiled=True)  19.5 us
    all_gather x1, waiting for transfers between devices, shards(): lax.all_gather(local_values, 'ctx', axis=2, tiled=True)  14.2 us
    dot_general x4, matrix products, absorb(): jnp.einsum('brn,bnd->brd', weights.astype(jnp.bfloat16), value_rows, pref...  10.4 us
    dot_general x1, matrix products, shards(): jnp.dot(lax.all_gather(rows_local, 'ctx', axis=0, tiled=True), out_weight...  8.94 us
    all_gather x1, waiting for transfers between devices, shards(): lax.all_gather(local_keys, 'ctx', axis=2, tiled=True)  8.13 us
    dot_general x4, matrix products, absorb(): jnp.einsum('brd,bnd->brn', queries, key_rows, preferred_element_type=jnp....  8.05 us
  transfers between devices with their start and end apart: 7, of which 7 were waited for; matrix products, arithmetic and copies ran while one was open for 6% of the time, Pallas kernels for 0%

profile of v1, /device:TPU:0, one launch (start us, length us, event | category | flops | bytes accessed | tf_op | source)
XLA Modules:
  0.0 223.3 jit_solution(764606031600318337)
XLA Ops:
  7.2 0.0 copy-start
  7.2 0.0 all-gather.4.cloned.1.call-start
  7.2 0.8 reshape.229
  8.1 0.2 copy-done
  8.2 1.6 gather_fusion
  9.8 0.0 copy-start.8
  9.8 0.0 copy-start.7
  9.9 2.7 %gather_fusion.1 = bf16[8,128,2,128]{3,2,1,0:T(2,128)(2,1)S(1)} fusion(bf16[8,128,2,128]{3,2,1,0:T(2,128)(2,1)} %param.17, s32[1024]{0:T(1024)S(1)} %pad_clamp_fusion), kind=kCustom, calls=%fused_computation.1.clone | custom fusion | bytes 1048608 | tf_op jit(solution)/shard_map/jit(_take)/gather | solution.py:110
  12.6 1.0 broadcast_select_fusion.1
  13.6 0.9 copy.131
  14.4 0.0 all-gather.4.cloned.1.call-update
  14.5 0.0 all-gather.6.cloned.1.call-start
  14.5 0.9 copy.130
  15.4 0.0 all-gather.6.cloned.1.call-update
  15.4 0.0 all-gather.8.cloned.1.call-start
  15.5 6.5 %all_gather.17 = bf16[2,128,2,128]{3,2,1,0:T(2,128)(2,1)S(1)} all-gather(bf16[2,32,2,128]{3,2,1,0:T(2,128)(2,1)S(1)} %copy-done.8), channel_id=1, replica_groups=mesh['groups'=2,'ctx'=4,'head'=4] {'ctx'}, dimensions={1}, use_global_device_ids=true | all-gather | bytes 163840 | tf_op jit(solution)/shard_map/all_gather | solution.py:120
  22.1 0.2 fusion.56
  22.3 5.9 %all_gather.18 = bf16[2,128,2,128]{3,2,1,0:T(2,128)(2,1)S(1)} all-gather(bf16[2,32,2,128]{3,2,1,0:T(2,128)(2,1)S(1)} %copy-done.9), channel_id=1, replica_groups=mesh['groups'=2,'ctx'=4,'head'=4] {'ctx'}, dimensions={1}, use_global_device_ids=true | all-gather | bytes 163840 | tf_op jit(solution)/shard_map/all_gather | solution.py:121
  28.3 0.7 reduce_max.56
  29.0 0.1 dynamic_slice.26
  29.1 0.6 iota_compare_fusion.2
  29.7 1.9 fusion.57
  31.7 0.2 fusion.58
  31.9 8.1 %all-gather.4.cloned.1.call-done = bf16[2,2,2048,128]{3,2,1,0:T(8,128)(2,1)} async-done(((bf16[2,2,512,128]{3,2,1,0:T(8,128)(2,1)}), bf16[2,2,2048,128]{3,2,1,0:T(8,128)(2,1)}) %all-gather.4.cloned.1.call-update) | async-done | bytes 2097168 | tf_op jit(solution)/shard_map/all_gather | solution.py:137
  40.0 2.8 %bitcast_reduce_fusion.1 = (f32[4,256]{1,0:T(4,128)S(1)}, f32[4,2048,256]{2,1,0:T(8,128)S(1)}) fusion(bf16[4,2048,128]{2,1,0:T(8,128)(2,1)} %bitcast.123, bf16[4,256,128]{2,1,0:T(8,128)(2,1)S(1)} %bitcast.133), kind=kOutput, calls=%fused_computation.6 | convolution fusion | flops 541064192 | bytes 10752000 | tf_op jit(solution)/shard_map/while/body/eval_jaxpr/brd,bnd->brn/dot_general | solution.py:22
  42.9 0.1 fusion.34
  43.0 1.4 fusion.2
  44.4 2.0 copy-done.1
  46.5 4.7 %bitcast_reduce_fusion = (f32[4,256]{1,0:T(4,128)S(1)}, f32[4,2048,256]{2,1,0:T(8,128)}) fusion(bf16[4,2048,128]{2,1,0:T(8,128)(2,1)S(1)} %bitcast.124, bf16[4,256,128]{2,1,0:T(8,128)(2,1)S(1)} %bitcast.131), kind=kOutput, calls=%fused_computation.3 | convolution fusion | flops 541064192 | bytes 10752000 | tf_op jit(solution)/shard_map/while/body/eval_jaxpr/brd,bnd->brn/dot_general | solution.py:22
  51.2 14.2 %all-gather.6.cloned.1.call-done = bf16[2,2,2048,128]{3,2,1,0:T(8,128)(2,1)} async-done(((bf16[2,2,512,128]{3,2,1,0:T(8,128)(2,1)}), bf16[2,2,2048,128]{3,2,1,0:T(8,128)(2,1)}) %all-gather.6.cloned.1.call-update) | async-done | bytes 2097168 | tf_op jit(solution)/shard_map/all_gather | solution.py:138
  65.4 5.2 %fusion.25 = f32[4,256,128]{2,1,0:T(8,128)S(1)} fusion(bf16[4,2048,128]{2,1,0:T(8,128)(2,1)} %bitcast.125, f32[4,2048,256]{2,1,0:T(8,128)} %copy-done.1, f32[4,256]{1,0:T(4,128)S(1)} %get-tuple-element.62, f32[4,256]{1,0:T(4,128)S(1)} %get-tuple-element.48, f32[4,256]{1,0:T(4,128)S(1)} %get-tuple-element.60), kind=kOutput, calls=%fused_computation.27 | convolution fusion | flops 543424512 | bytes 11022336 | tf_op jit(solution)/shard_map/while/body/eval_jaxpr/brn,bnd->brd/dot_general | solution.py:31
  70.6 0.3 fusion.28
  70.9 0.1 reshape.239
  71.1 0.6 fusion.54
  71.7 0.7 max.91
  72.4 4.9 %fusion.4 = f32[4,256]{1,0:T(4,128)S(1)} fusion(f32[4,2048,256]{2,1,0:T(8,128)} %get-tuple-element.84, f32[4,256]{1,0:T(4,128)S(1)} %get-tuple-element.71), kind=kLoop, calls=%fused_computation.10 | loop fusion | flops 6290432 | bytes 8396800 | tf_op jit(solution)/shard_map/while/body/eval_jaxpr/reduce_sum | solution.py:30
  77.3 0.7 reduce_sum.94
  78.0 0.1 fusion.36
  78.1 0.7 reduce_sum.96
  78.8 1.0 select_reduce_fusion.1
  79.9 0.8 copy_maximum_fusion
  80.6 1.0 fusion.43
  81.7 0.8 bitcast_add_fusion
  82.5 4.6 %fusion.22 = f32[4,256,128]{2,1,0:T(8,128)S(1)} fusion(bf16[4,2048,128]{2,1,0:T(8,128)(2,1)S(1)} %bitcast.126, f32[4,2048,256]{2,1,0:T(8,128)} %get-tuple-element.84, f32[4,256]{1,0:T(4,128)S(1)} %get-tuple-element.71, f32[4,256]{1,0:T(4,128)S(1)} %get-tuple-element.59, f32[4,256]{1,0:T(4,128)} %get-tuple-element.70), kind=kOutput, calls=%fused_computation.26 | convolution fusion | flops 543424512 | bytes 11022336 | tf_op jit(solution)/shard_map/while/body/eval_jaxpr/brn,bnd->brd/dot_general | solution.py:31
  87.1 0.3 convolution_add_fusion
  87.4 0.1 select_reduce_fusion
  87.5 0.3 fusion.31
  87.9 0.1 reshape.243
  88.0 0.8 pad_maximum_fusion
  88.7 0.0 all-gather.8.cloned.1.call-update
  88.8 0.3 reduce-scatter.2.cloned.1.call-start
  89.0 19.5 %all-gather.8.cloned.1.call-done = bf16[384,2048]{1,0:T(8,128)(2,1)} async-done(((bf16[96,2048]{1,0:T(8,128)(2,1)}), bf16[384,2048]{1,0:T(8,128)(2,1)}) %all-gather.8.cloned.1.call-update) | async-done | bytes 1572880 | tf_op jit(solution)/shard_map/all_gather | solution.py:178
  108.6 8.9 %fusion.59 = f32[384,2048]{1,0:T(8,128)} fusion(bf16[384,2048]{1,0:T(8,128)(2,1)} %all-gather.8.cloned.1.call-done, bf16[2048,2048]{1,0:T(8,128)(2,1)} %param.23), kind=kOutput, calls=%fused_computation.102 | convolution fusion | flops 3221225472 | bytes 13107200 | tf_op jit(solution)/shard_map/dot_general | solution.py:177
  117.5 0.0 reduce-scatter.2.cloned.1.call-update
  117.5 60.4 %reduce-scatter.2.cloned.1.call-done = f32[96,2048]{1,0:T(8,128)} async-done(((f32[384,2048]{1,0:T(8,128)}), f32[96,2048]{1,0:T(8,128)}) %reduce-scatter.2.cloned.1.call-update) | async-done | bytes 786448 | tf_op jit(solution)/shard_map/reduce_scatter | solution.py:182
  178.0 1.2 convert_element_type.35
  179.2 1.1 collective-permute-start
  180.3 11.5 %collective-permute-done = bf16[96,2048]{1,0:T(8,128)(2,1)S(1)} collective-permute-done((bf16[96,2048]{1,0:T(8,128)(2,1)S(1)}, bf16[96,2048]{1,0:T(8,128)(2,1)S(1)}, u32[]{:S(2)}, u32[]{:S(2)}) %collective-permute-start) | collective-permute-done | bytes 393248 | tf_op jit(solution)/shard_map/ppermute | solution.py:14
  191.8 11.6 %collective-permute-done.1 = bf16[96,2048]{1,0:T(8,128)(2,1)S(1)} collective-permute-done((bf16[96,2048]{1,0:T(8,128)(2,1)S(1)}, bf16[96,2048]{1,0:T(8,128)(2,1)S(1)}, u32[]{:S(2)}, u32[]{:S(2)}) %collective-permute-start.1) | collective-permute-done | bytes 393248 | tf_op jit(solution)/shard_map/ppermute | solution.py:14
  203.4 10.7 %collective-permute-done.2 = bf16[96,2048]{1,0:T(8,128)(2,1)S(1)} collective-permute-done((bf16[96,2048]{1,0:T(8,128)(2,1)S(1)}, bf16[96,2048]{1,0:T(8,128)(2,1)S(1)}, u32[]{:S(2)}, u32[]{:S(2)}) %collective-permute-start.2) | collective-permute-done | bytes 393248 | tf_op jit(solution)/shard_map/ppermute | solution.py:14
  214.3 0.5 constant_dynamic-slice_fusion
  214.8 0.1 slice.12
  214.9 0.8 copy_bitcast_fusion
  215.7 1.0 copy.99
  (51 shorter events, 0.6 us)
Async XLA Ops:
  7.2 1.1 copy-start
  7.2 32.9 %all-gather.4.cloned.1.call-start = ((), (), s32[]{:S(2)}) async-start(), calls=%async_computation.1 | async-start | bytes 2621440 | tf_op jit(solution)/shard_map/all_gather | solution.py:137
  9.8 5.6 %copy-start.8 = (bf16[2,32,2,128]{3,2,1,0:T(2,128)(2,1)S(1)}, bf16[2,32,2,128]{3,2,1,0:T(2,128)(2,1)}, u32[]{:S(2)}) copy-start(bf16[2,32,2,128]{3,2,1,0:T(2,128)(2,1)} %param.14) | copy-start | bytes 98308
  9.8 12.1 %copy-start.7 = (bf16[4,8,16,128]{3,2,1,0:T(8,128)(2,1)S(1)}, bf16[4,8,16,128]{3,2,1,0:T(8,128)(2,1)}, u32[]{:S(2)}) copy-start(bf16[4,8,16,128]{3,2,1,0:T(8,128)(2,1)} %param.19) | copy-start | bytes 393220
  12.5 9.8 %copy-start.9 = (bf16[2,32,2,128]{3,2,1,0:T(2,128)(2,1)S(1)}, bf16[2,32,2,128]{3,2,1,0:T(2,128)(2,1)}, u32[]{:S(2)}) copy-start(bf16[2,32,2,128]{3,2,1,0:T(2,128)(2,1)} %param.15) | copy-start | bytes 98308
  13.5 14.7 %copy-start.5 = (bf16[2,32,16,128]{3,2,1,0:T(8,128)(2,1)S(1)}, bf16[2,32,16,128]{3,2,1,0:T(8,128)(2,1)}, u32[]{:S(2)}) copy-start(bf16[2,32,16,128]{3,2,1,0:T(8,128)(2,1)} %param.13) | copy-start | bytes 786436
  13.6 15.5 %copy-start.13 = (s32[32]{0:T(128)S(1)}, s32[32]{0:T(128)}, u32[]{:S(2)}) copy-start(s32[32]{0:T(128)} %param.22) | copy-start | bytes 388
  13.6 16.1 %copy-start.11 = (bf16[4,8,2,128]{3,2,1,0:T(2,128)(2,1)S(1)}, bf16[4,8,2,128]{3,2,1,0:T(2,128)(2,1)}, u32[]{:S(2)}) copy-start(bf16[4,8,2,128]{3,2,1,0:T(2,128)(2,1)} %param.20) | copy-start | bytes 49156
  14.5 50.9 %all-gather.6.cloned.1.call-start = ((), (), s32[]{:S(2)}) async-start(), calls=%async_computation.2 | async-start | bytes 2621440 | tf_op jit(solution)/shard_map/all_gather | solution.py:138
  15.4 93.2 %all-gather.8.cloned.1.call-start = ((), (), s32[]{:S(2)}) async-start(), calls=%async_computation.3 | async-start | bytes 1966080 | tf_op jit(solution)/shard_map/all_gather | solution.py:178
  42.9 3.6 %copy-start.1 = (f32[4,2048,256]{2,1,0:T(8,128)}, f32[4,2048,256]{2,1,0:T(8,128)S(1)}, u32[]{:S(2)}) copy-start(f32[4,2048,256]{2,1,0:T(8,128)S(1)} %get-tuple-element.88) | copy-start | bytes 25165828
  43.0 3.5 %copy-start.2 = (bf16[2,2,2048,128]{3,2,1,0:T(8,128)(2,1)S(1)}, bf16[2,2,2048,128]{3,2,1,0:T(8,128)(2,1)}, u32[]{:S(2)}) copy-start(bf16[2,2,2048,128]{3,2,1,0:T(8,128)(2,1)} %all-gather.4.cloned.1.call-done) | copy-start | bytes 6291460
  72.4 10.1 %copy-start.3 = (bf16[2,2,2048,128]{3,2,1,0:T(8,128)(2,1)S(1)}, bf16[2,2,2048,128]{3,2,1,0:T(8,128)(2,1)}, u32[]{:S(2)}) copy-start(bf16[2,2,2048,128]{3,2,1,0:T(8,128)(2,1)} %all-gather.6.cloned.1.call-done) | copy-start | bytes 6291460
  82.5 4.9 %copy-start.10 = (pred[2,8]{1,0:T(4,128)(4,1)S(1)}, pred[2,8]{1,0:T(4,128)(4,1)}, u32[]{:S(2)}) copy-start(pred[2,8]{1,0:T(4,128)(4,1)} %iota_compare_fusion.2) | copy-start | bytes 52
  82.5 5.0 %copy-start.6 = (f32[2,4,8,8,4]{3,4,1,2,0:T(4,128)S(1)}, f32[2,4,8,8,4]{3,4,1,2,0:T(4,128)}, u32[]{:S(2)}) copy-start(f32[2,4,8,8,4]{3,4,1,2,0:T(4,128)} %get-tuple-element.86) | copy-start | bytes 24580
  82.5 5.0 %copy-start.12 = (bf16[4,8,2,128]{3,2,1,0:T(2,128)(2,1)S(1)}, bf16[4,8,2,128]{3,2,1,0:T(2,128)(2,1)}, u32[]{:S(2)}) copy-start(bf16[4,8,2,128]{3,2,1,0:T(2,128)(2,1)} %param.21) | copy-start | bytes 49156
  88.8 89.2 %reduce-scatter.2.cloned.1.call-start = ((), (), s32[]{:S(2)}) async-start(), calls=%async_computation.4 | async-start | bytes 3932160 | tf_op jit(solution)/shard_map/reduce_scatter | solution.py:182
  177.9 36.2 %copy-start.4 = (f32[96,2048]{1,0:T(8,128)S(1)}, f32[96,2048]{1,0:T(8,128)}, u32[]{:S(2)}) copy-start(f32[96,2048]{1,0:T(8,128)} %reduce-scatter.2.cloned.1.call-done) | copy-start | bytes 2359300
  179.2 12.5 %collective-permute-start = (bf16[96,2048]{1,0:T(8,128)(2,1)S(1)}, bf16[96,2048]{1,0:T(8,128)(2,1)S(1)}, u32[]{:S(2)}, u32[]{:S(2)}) collective-permute-start(bf16[96,2048]{1,0:T(8,128)(2,1)S(1)} %convert_element_type.35), channel_id=1, source_target_pairs={{0,1},{1,2},{2,3},{3,0},{4,5},{5,6},{6,7},{7,4},{8,9},{9,10},{10,1... | collective-permute-start | bytes 1179656 | tf_op jit(solution)/shard_map/ppermute | solution.py:14
  191.8 11.6 %collective-permute-start.1 = (bf16[96,2048]{1,0:T(8,128)(2,1)S(1)}, bf16[96,2048]{1,0:T(8,128)(2,1)S(1)}, u32[]{:S(2)}, u32[]{:S(2)}) collective-permute-start(bf16[96,2048]{1,0:T(8,128)(2,1)S(1)} %collective-permute-done), channel_id=1, source_target_pairs={{0,1},{1,2},{2,3},{3,0},{4,5},{5,6},{6,7},{7,4},{8,9},{9,10},{10,1... | collective-permute-start | bytes 1179656 | tf_op jit(solution)/shard_map/ppermute | solution.py:14
  203.3 10.7 %collective-permute-start.2 = (bf16[96,2048]{1,0:T(8,128)(2,1)S(1)}, bf16[96,2048]{1,0:T(8,128)(2,1)S(1)}, u32[]{:S(2)}, u32[]{:S(2)}) collective-permute-start(bf16[96,2048]{1,0:T(8,128)(2,1)S(1)} %collective-permute-done.1), channel_id=1, source_target_pairs={{0,1},{1,2},{2,3},{3,0},{4,5},{5,6},{6,7},{7,4},{8,9},{9,10},{10,1... | collective-permute-start | bytes 1179656 | tf_op jit(solution)/shard_map/ppermute | solution.py:14
Sparse Core Ops, SparseCore 0:
  14.6 25.4 all-gather.3
  42.2 23.1 all-gather.5
  88.9 19.6 all-gather.7
  117.7 60.2 reduce-scatter.1
